TPU v7x, 256 devices: a whole 4x4x8 slice. The times are simulated.
256 devices in a mesh: dp: 64 (over x, z, core), tensor: 4 (over y).
Axes of the slice: x: 4, y: 4, z: 8, core: 2. Of those that a mesh axis runs over, the one named last changes fastest.
Arguments:
- tokens: bfloat16 [512, 16384], P('dp', 'tensor'), may hold values from -6 to 6
- clip_act: float32 [16384], P('tensor'), may hold values from 0.5 to 4
- weight: bfloat16 [16384, 49152], P('tensor', 'dp'), may hold values from -0.046875 to 0.046875
- clip_weight: float32 [49152], P('dp'), may hold values from 0.003 to 0.03
- cotangent: bfloat16 [512, 49152], P('tensor', 'dp'), may hold values from -16 to 16
Outputs:
- projected: bfloat16 [512, 49152], P('tensor', 'dp')
- token_grad: bfloat16 [512, 16384], P('dp', 'tensor')
- weight_grad: bfloat16 [16384, 49152], P('tensor', 'dp')
- clip_act_grad: float32 [16384], P('tensor')
- clip_weight_grad: float32 [49152], P('dp')
All inputs are finite; a program needn't handle non-finite values.
Results may differ from a plain program's by a relative error of at most 0.009.
Values may be sent and summed in bfloat16 or wider, within the bound.
No kernel may reach another device: no remote copies, remote signals or barrier semaphores. Data moves between devices by JAX's collectives and lax.ppermute only.
A program may use at most 128 MiB of HBM per device.

v0:
```python
import math
import jax
import jax.numpy as jnp
from jax import lax
from jax.sharding import PartitionSpec as P


def swapped(block, axis, bit):
    count = lax.axis_size(axis)
    route = []
    for low in range(count):
        high = low | 1 << bit
        if high != low and high < count:
            route += [(low, high), (high, low)]
    return lax.ppermute(block, axis, route)


def sylvester(order):
    index = lax.iota(jnp.int32, order)
    joined = jnp.bitwise_and(index[:, None], index[None, :])
    parity = jnp.zeros((order, order), jnp.int32)
    for bit_number in range(max(order.bit_length() - 1, 0)):
        parity = parity + jnp.bitwise_and(jnp.right_shift(joined, bit_number), 1)
    return (1 - 2 * jnp.bitwise_and(parity, 1)).astype(jnp.float32)


def local_rotate(values, norm_factor):
    row_total, width = values.shape
    levels = width.bit_length() - 1
    outer = 2 ** (levels // 2)
    inner = width // outer
    blocks = values.reshape(row_total, outer, inner)
    blocks = jnp.einsum("rab,ac->rcb", blocks, sylvester(outer), precision=lax.Precision.HIGHEST)
    blocks = jnp.einsum("rcb,bd->rcd", blocks, sylvester(inner), precision=lax.Precision.HIGHEST)
    return blocks.reshape(row_total, width) * norm_factor


def rotate(values):
    group_size = lax.axis_size("tensor")
    norm_factor = 1.0 / math.sqrt(values.shape[1] * group_size)
    mixed = local_rotate(values, norm_factor)
    position = lax.axis_index("tensor")
    for bit_number in range(group_size.bit_length() - 1):
        partner = swapped(mixed, "tensor", bit_number)
        upper = jnp.bitwise_and(jnp.right_shift(position, bit_number), 1) == 1
        mixed = jnp.where(upper, partner - mixed, mixed + partner)
    return mixed


def body(tokens, clip_act, weight, clip_weight, cotangent):
    rotated = rotate(tokens.astype(jnp.float32))
    ratio_act = rotated / clip_act
    tanh_act = jnp.tanh(ratio_act)
    quant_act = (clip_act * tanh_act).astype(jnp.bfloat16)
    slope_act = 1.0 - tanh_act * tanh_act
    edge_act = tanh_act - ratio_act * slope_act
    rows, width = quant_act.shape
    chips = lax.axis_size("dx") * lax.axis_size("dz")
    cores = lax.axis_size("dc")
    core = lax.axis_index("dc")
    ratio_weight = weight.astype(jnp.float32) / clip_weight
    tanh_weight = jnp.tanh(ratio_weight)
    quant_weight = (clip_weight * tanh_weight).astype(jnp.bfloat16)
    all_cot = lax.all_gather(cotangent, "tensor", axis=0, tiled=True)
    partial = lax.dot_general(
        all_cot, quant_weight, (((1,), (1,)), ((), ())), preferred_element_type=jnp.float32
    ).reshape(chips, cores, rows, width)
    quant_act, partial = lax.optimization_barrier((quant_act, partial))
    half_act = lax.all_gather(quant_act, CHIPS, axis=0, tiled=True)
    pair = [(0, 1), (1, 0)]
    partner_act = lax.ppermute(half_act, "dc", pair)
    both_act = jnp.where(
        core == 0, jnp.stack([half_act, partner_act]), jnp.stack([partner_act, half_act])
    )
    all_act = both_act.reshape(cores, chips, rows, width).transpose(1, 0, 2, 3).reshape(-1, width)
    block = all_act
    projected = lax.psum_scatter(
        jnp.dot(block, quant_weight, preferred_element_type=jnp.float32),
        "tensor",
        scatter_dimension=0,
        tiled=True,
    ).astype(jnp.bfloat16)
    weight_prod = lax.dot_general(
        all_act, all_cot, (((0,), (0,)), ((), ())), preferred_element_type=jnp.float32
    )
    slope_weight = 1.0 - tanh_weight * tanh_weight
    weight_grad = (weight_prod * slope_weight).astype(jnp.bfloat16)
    weight_terms = jnp.sum(weight_prod * (tanh_weight - ratio_weight * slope_weight), axis=0)
    clip_weight_grad = lax.psum(weight_terms, "tensor")
    mine = lax.dynamic_index_in_dim(partial, core, axis=1, keepdims=False)
    other = lax.dynamic_index_in_dim(partial, cores - 1 - core, axis=1, keepdims=False)
    chip_sum = mine + lax.ppermute(other.astype(jnp.bfloat16), "dc", pair).astype(jnp.float32)
    pieces = lax.all_to_all(chip_sum.astype(jnp.bfloat16), CHIPS, 0, 0, tiled=True)
    act_prod = jnp.sum(pieces.astype(jnp.float32), axis=0)
    act_terms = jnp.sum(act_prod * edge_act, axis=0)
    groups = lax.axis_size("tensor")
    slots = jnp.zeros((groups,) + act_terms.shape, act_terms.dtype)
    slots = lax.dynamic_update_index_in_dim(slots, act_terms, lax.axis_index("tensor"), 0)
    slots = lax.psum(slots, DP + ("tensor",))
    clip_act_grad = lax.dynamic_index_in_dim(slots, lax.axis_index("tensor"), 0, keepdims=False)
    pre_rotation = act_prod * slope_act
    token_grad = rotate(pre_rotation).astype(jnp.bfloat16)
    return (projected, token_grad, weight_grad, clip_act_grad, clip_weight_grad)


DP = ("dx", "dz", "dc")
CHIPS = ("dx", "dz")


def solution(mesh):
    rows, cols = mesh.devices.shape
    cores = 2
    across = 4 if rows % (4 * cores) == 0 else 1
    grid = mesh.devices.reshape(across, rows // (across * cores), cores, cols)
    fine = jax.sharding.Mesh(grid, ("dx", "dz", "dc", "tensor"))
    in_specs = (P(DP, "tensor"), P("tensor"), P("tensor", DP), P(DP), P("tensor", DP))
    out_specs = (P("tensor", DP), P(DP, "tensor"), P("tensor", DP), P("tensor"), P(DP))
    return jax.shard_map(body, mesh=fine, in_specs=in_specs, out_specs=out_specs, check_vma=False)
```

profile of v0, /device:TPU:1, one launch (start us, length us, event | category | flops | bytes accessed | tf_op | source)
XLA Modules:
  0.0 391.6 jit_solution(14210989227953233177)
XLA Ops:
  8.0 0.0 all-gather.2.cloned.1.call-start
  8.0 1.0 reshape.40
  9.1 0.3 convolution_bitcast_fusion.1
  9.4 0.4 convolution_multiply_fusion.1
  9.8 0.1 mul.67
  9.9 0.0 copy-start.2
  9.9 2.2 collective-permute-start
  12.1 7.3 %multiply_convert_fusion.1 = bf16[4096,768]{1,0:T(8,128)(2,1)} fusion(f32[768]{0:T(1024)} %param.8, bf16[4096,768]{1,0:T(8,128)(2,1)} %param.7), kind=kLoop, calls=%fused_computation.3 | loop fusion | flops 12582912 | bytes 12585984 | tf_op jit(solution)/shard_map/convert_element_type | solution.py:63
  19.4 0.0 copy-done.2
  19.4 11.8 %all_gather.6 = bf16[512,768]{1,0:T(8,128)(2,1)S(1)} all-gather(bf16[128,768]{1,0:T(8,128)(2,1)S(1)} %copy-done.2), channel_id=1, replica_groups=mesh['dx'=4,'dz'=8,'dc'=2,'tensor'=4] {'tensor'}, dimensions={0}, use_global_device_ids=true | all-gather | bytes 983040 | tf_op jit(solution)/shard_map/all_gather | solution.py:64
  31.2 0.0 collective-permute-done
  31.2 0.0 copy-start.3
  31.2 1.3 collective-permute-start.1
  32.5 8.4 %fusion.35 = f32[4096,512]{0,1:T(8,128)} fusion(bf16[4096,768]{1,0:T(8,128)(2,1)} %multiply_convert_fusion.1, bf16[512,768]{1,0:T(8,128)(2,1)S(1)} %all_gather.6), kind=kOutput, calls=%fused_computation.57 | convolution fusion | flops 3221225472 | bytes 15466496 | tf_op jit(solution)/shard_map/dot_general | solution.py:65
  40.9 0.0 collective-permute-done.1
  40.9 0.0 copy-done.3
  40.9 0.7 multiply_convert_fusion.2
  41.6 2.5 fusion.1
  44.1 3.5 collective-permute-start.3
  47.6 0.0 all-gather.2.cloned.1.call-update
  47.6 3.9 collective-permute-done.3
  51.5 4.7 %fusion = bf16[32,8,4096]{2,1,0:T(8,128)(2,1)} fusion(bf16[32,8,4096]{2,1,0:T(8,128)(2,1)} %collective-permute-done.3, f32[32,2,8,4096]{3,2,1,0:T(8,128)} %bitcast.40, s32[]{:T(128)S(6)} %select_n.50), kind=kLoop, calls=%fused_computation.7 | loop fusion | flops 3145728 | bytes 8388612 | tf_op jit(solution)/shard_map/convert_element_type | solution.py:93
  56.3 11.0 %all-to-all-start = ((bf16[32,8,4096]{2,1,0:T(8,128)(2,1)}), bf16[32,8,4096]{2,1,0:T(8,128)(2,1)S(1)}, u32[]{:S(2)}, u32[]{:S(2)}) async-start(bf16[32,8,4096]{2,1,0:T(8,128)(2,1)} %fusion), calls=%async_computation.1 | async-start | bytes 4194304 | tf_op jit(solution)/shard_map/all_to_all | solution.py:93
  67.3 0.0 all-reduce.2.cloned.1.call-start
  67.4 66.5 %all-gather.2.cloned.1.call-done = bf16[256,4096]{1,0:T(8,128)(2,1)} async-done(((bf16[8,4096]{1,0:T(8,128)(2,1)}), bf16[256,4096]{1,0:T(8,128)(2,1)}) %all-gather.2.cloned.1.call-update) | async-done | bytes 2097168 | tf_op jit(solution)/shard_map/all_gather | solution.py:69
  133.8 2.7 collective-permute-start.2
  136.5 0.0 all-to-all-done
  136.5 0.3 convert_reduce_fusion
  136.8 0.1 multiply_reduce_fusion.1
  136.9 0.1 reshape.43
  137.0 0.4 convolution_bitcast_fusion
  137.4 0.4 convolution_multiply_fusion
  137.8 0.1 mul.74
  137.9 1.3 collective-permute-start.4
  139.2 0.2 dynamic_update_slice.4
  139.5 0.0 copy-start.1
  139.5 0.6 copy-done.1
  140.1 0.0 all-reduce.2.cloned.1.call-update
  140.2 0.2 reduce-scatter.2.cloned.1.call-start
  140.4 0.3 collective-permute-done.2
  140.7 4.1 %maximum_select_fusion = bf16[2,32,8,4096]{3,2,0,1:T(8,128)(2,1)S(1)} fusion(bf16[1,32,8,4096]{3,2,0,1:T(8,128)(2,1)} %bitcast.5, bf16[1,32,8,4096]{3,2,0,1:T(8,128)(2,1)} %bitcast.43, pred[]{:T(512)S(6)} %eq.11), kind=kLoop, calls=%fused_computation.5 | loop fusion | flops 6291456 | bytes 8388609 | tf_op jit(solution)/shard_map/jit(_where)/select_n | solution.py:72
  144.7 0.0 copy-start
  144.7 1.9 copy-done
  146.7 0.0 copy-start.4
  146.7 6.7 %fusion.36 = f32[512,768]{1,0:T(8,128)} fusion(bf16[512,4096]{1,0:T(8,128)(2,1)S(1)} %bitcast.41, bf16[4096,768]{1,0:T(8,128)(2,1)} %multiply_convert_fusion.1), kind=kOutput, calls=%fused_computation.58 | convolution fusion | flops 3221225472 | bytes 12058624 | tf_op jit(solution)/shard_map/dot_general | solution.py:78
  153.3 0.0 reduce-scatter.2.cloned.1.call-update
  153.4 0.0 copy-done.4
  153.4 12.5 %multiply_reduce_fusion = (f32[768]{0:T(1024)S(1)}, bf16[4096,768]{1,0:T(8,128)(2,1)}) fusion(f32[768]{0:T(1024)S(1)} %copy-done.4, bf16[4096,768]{1,0:T(8,128)(2,1)} %param.7, bf16[512,4096]{1,0:T(8,128)(2,1)} %bitcast.42, bf16[512,768]{1,0:T(8,128)(2,1)S(1)} %all_gather.6), kind=kOutput, calls=%fused_computation | convolution fusion | flops 3252681984 | bytes 17569792 | tf_op jit(solution)/shard_map/dot_general | solution.py:83
  165.8 10.0 %psum.15 = f32[768]{0:T(1024)} all-reduce(f32[768]{0:T(1024)S(1)} %get-tuple-element.11), channel_id=1, replica_groups=mesh['dx'=4,'dz'=8,'dc'=2,'tensor'=4] {'tensor'}, use_global_device_ids=true, to_apply=%region_5.6 | all-reduce | flops 768 | bytes 6144 | tf_op jit(solution)/shard_map/psum | solution.py:89
  175.8 0.0 collective-permute-done.4
  175.8 0.7 collective-permute-start.5
  176.5 203.9 %all-reduce.2.cloned.1.call-done = f32[4,4096]{1,0:T(4,128)} async-done(((f32[4,4096]{1,0:T(4,128)}), f32[4,4096]{1,0:T(4,128)}) %all-reduce.2.cloned.1.call-update) | async-done | bytes 65552 | tf_op jit(solution)/shard_map/psum | solution.py:99
  380.4 1.5 constant_dynamic-slice_fusion
  381.8 0.0 collective-permute-done.5
  381.8 0.6 select_convert_fusion
  382.5 0.0 reduce-scatter.2.cloned.1.call-done
  382.5 1.7 convert_element_type.50
  (3 shorter events, 0.0 us)
Async XLA Ops:
  8.0 125.8 %all-gather.2.cloned.1.call-start = ((), (), s32[]{:S(2)}) async-start(), calls=%async_computation.2 | async-start | bytes 2162688 | tf_op jit(solution)/shard_map/all_gather | solution.py:69
  9.9 9.5 %copy-start.2 = (bf16[128,768]{1,0:T(8,128)(2,1)S(1)}, bf16[128,768]{1,0:T(8,128)(2,1)}, u32[]{:S(2)}) copy-start(bf16[128,768]{1,0:T(8,128)(2,1)} %param.9) | copy-start | bytes 589828
  9.9 21.3 %collective-permute-start = (f32[8,4096]{1,0:T(8,128)S(1)}, f32[8,4096]{1,0:T(8,128)S(1)}, u32[]{:S(2)}, u32[]{:S(2)}) collective-permute-start(f32[8,4096]{1,0:T(8,128)S(1)} %mul.67), channel_id=1, source_target_pairs={{0,1},{1,0},{2,3},{3,2},{4,5},{5,4},{6,7},{7,6},{8,9},{9,8},{10,11... | collective-permute-start | bytes 393224 | tf_op jit(solution)/shard_map/ppermute | solution.py:15
  31.2 9.7 %copy-start.3 = (f32[4096]{0:T(1024)S(1)}, f32[4096]{0:T(1024)}, u32[]{:S(2)}) copy-start(f32[4096]{0:T(1024)} %param.6) | copy-start | bytes 49156
  31.2 9.7 %collective-permute-start.1 = (f32[8,4096]{1,0:T(8,128)S(1)}, f32[8,4096]{1,0:T(8,128)S(1)}, u32[]{:S(2)}, u32[]{:S(2)}) collective-permute-start(f32[8,4096]{1,0:T(8,128)S(1)} %add_select_fusion.1), channel_id=1, source_target_pairs={{0,2},{2,0},{1,3},{3,1},{4,6},{6,4},{5,7},{7,5},{8,10},{10,8},{9,1... | collective-permute-start | bytes 393224 | tf_op jit(solution)/shard_map/ppermute | solution.py:15
  44.1 7.4 %collective-permute-start.3 = (bf16[32,8,4096]{2,1,0:T(8,128)(2,1)S(1)}, bf16[32,8,4096]{2,1,0:T(8,128)(2,1)}, u32[]{:S(2)}, u32[]{:S(2)}) collective-permute-start(bf16[32,8,4096]{2,1,0:T(8,128)(2,1)S(1)} %fusion.1), channel_id=1, source_target_pairs={{0,4},{4,0},{1,5},{5,1},{2,6},{6,2},{3,7},{7,3},{8,12},{12,8},{9,1... | collective-permute-start | bytes 6291464 | tf_op jit(solution)/shard_map/ppermute | solution.py:92
  56.3 80.3 %all-to-all-start = ((bf16[32,8,4096]{2,1,0:T(8,128)(2,1)}), bf16[32,8,4096]{2,1,0:T(8,128)(2,1)S(1)}, u32[]{:S(2)}, u32[]{:S(2)}) async-start(bf16[32,8,4096]{2,1,0:T(8,128)(2,1)} %fusion), calls=%async_computation.1 | async-start | bytes 4194304 | tf_op jit(solution)/shard_map/all_to_all | solution.py:93
  67.3 313.1 %all-reduce.2.cloned.1.call-start = ((), (), s32[]{:S(2)}) async-start(), calls=%async_computation.4 | async-start | bytes 131072 | tf_op jit(solution)/shard_map/psum | solution.py:99
  133.8 6.8 %collective-permute-start.2 = (bf16[256,4096]{1,0:T(8,128)(2,1)}, bf16[256,4096]{1,0:T(8,128)(2,1)}, u32[]{:S(2)}, u32[]{:S(2)}) collective-permute-start(bf16[256,4096]{1,0:T(8,128)(2,1)} %all-gather.2.cloned.1.call-done), channel_id=1, source_target_pairs={{0,4},{4,0},{1,5},{5,1},{2,6},{6,2},{3,7},{7,3},{8,12},{12,8},{9,1... | collective-permute-start | bytes 6291464 | tf_op jit(solution)/shard_map/ppermute | solution.py:71
  137.9 37.9 %collective-permute-start.4 = (f32[8,4096]{1,0:T(8,128)S(1)}, f32[8,4096]{1,0:T(8,128)S(1)}, u32[]{:S(2)}, u32[]{:S(2)}) collective-permute-start(f32[8,4096]{1,0:T(8,128)S(1)} %mul.74), channel_id=1, source_target_pairs={{0,1},{1,0},{2,3},{3,2},{4,5},{5,4},{6,7},{7,6},{8,9},{9,8},{10,11... | collective-permute-start | bytes 393224 | tf_op jit(solution)/shard_map/ppermute | solution.py:15
  139.5 0.6 copy-start.1
  140.2 242.3 %reduce-scatter.2.cloned.1.call-start = ((), (), s32[]{:S(2)}) async-start(), calls=%async_computation.3 | async-start | bytes 1966080 | tf_op jit(solution)/shard_map/reduce_scatter | solution.py:77
  144.7 1.9 copy-start
  146.7 6.7 %copy-start.4 = (f32[768]{0:T(1024)S(1)}, f32[768]{0:T(1024)}, u32[]{:S(2)}) copy-start(f32[768]{0:T(1024)} %param.8) | copy-start | bytes 9220
  175.8 206.0 %collective-permute-start.5 = (f32[8,4096]{1,0:T(8,128)S(1)}, f32[8,4096]{1,0:T(8,128)S(1)}, u32[]{:S(2)}, u32[]{:S(2)}) collective-permute-start(f32[8,4096]{1,0:T(8,128)S(1)} %add_select_fusion), channel_id=1, source_target_pairs={{0,2},{2,0},{1,3},{3,1},{4,6},{6,4},{5,7},{7,5},{8,10},{10,8},{9,1... | collective-permute-start | bytes 393224 | tf_op jit(solution)/shard_map/ppermute | solution.py:15
Sparse Core Ops, SparseCore 0:
  47.8 86.0 all-gather.1
  153.5 26.5 reduce-scatter.1
Sparse Core Ops, SparseCore 1:
  140.2 240.1 all-reduce.1
where the time goes:
time: 392 us
  waiting for transfers between devices  275 us (70%)
  matrix products  29.1 us (7%)
  starting transfers between devices  23 us (6%)
  blocking collectives  21.8 us (6%)
  other arithmetic  19.5 us (5%)
  between operations  15.6 us (4%)
  local copies, waits for them, and re-layouts  8.11 us (2%)
    psum x1, waiting for transfers between devices, body(): slots = lax.psum(slots, DP + ('tensor',))  204 us
    all_gather x1, waiting for transfers between devices, body(): half_act = lax.all_gather(quant_act, CHIPS, axis=0, tiled=True)  66.5 us
    dot_general x1, matrix products, body(): lax.dot_general(all_act, all_cot, (((0,), (0,)), ((), ())), preferred_ele...  12.5 us
    all_gather x1, blocking collectives, body(): all_cot = lax.all_gather(cotangent, 'tensor', axis=0, tiled=True)  11.8 us
    all_to_all x1, starting transfers between devices, body(): lax.all_to_all(chip_sum.astype(jnp.bfloat16), CHIPS, 0, 0, tiled=True)  11 us
    psum x1, blocking collectives, body(): clip_weight_grad = lax.psum(weight_terms, 'tensor')  9.99 us
    dot_general x1, matrix products, body(): lax.dot_general(all_cot, quant_weight, (((1,), (1,)), ((), ())), preferre...  8.43 us
  transfers between devices with their start and end apart: 10, of which 4 were waited for; matrix products, arithmetic and copies ran while one was open for 12% of the time, Pallas kernels for 0%

commit v1 on v0

--- a/solution.py
+++ b/solution.py
@@ -96,7 +96,7 @@
     groups = lax.axis_size("tensor")
     slots = jnp.zeros((groups,) + act_terms.shape, act_terms.dtype)
     slots = lax.dynamic_update_index_in_dim(slots, act_terms, lax.axis_index("tensor"), 0)
-    slots = lax.psum(slots, DP + ("tensor",))
+    slots = jnp.sum(lax.all_gather(slots, DP + ("tensor",)), axis=0)
     clip_act_grad = lax.dynamic_index_in_dim(slots, lax.axis_index("tensor"), 0, keepdims=False)
     pre_rotation = act_prod * slope_act
     token_grad = rotate(pre_rotation).astype(jnp.bfloat16)

time: 392 us -> 328 us (0.84)
  waiting for transfers between devices: 275 us -> 205 us
  other arithmetic: 19.5 us -> 28.5 us
    psum x1 -> x0, waiting for transfers between devices: 204 us -> none  [body(): slots = lax.psum(slots, DP + ('tensor',))]
    all_gather x0 -> x1, waiting for transfers between devices: none -> 94.3 us  [body(): slots = jnp.sum(lax.all_gather(slots, DP + ('tensor',)), axis=0)]
    all_to_all x1, waiting for transfers between devices: 0.01 us -> 36.2 us  [body(): lax.all_to_all(chip_sum.astype(jnp.bfloat16), CHIPS, 0, 0, tiled=True)]
    reduce_sum x0 -> x1, other arithmetic: none -> 8.81 us  [body(): slots = jnp.sum(lax.all_gather(slots, DP + ('tensor',)), axis=0)]
    all_gather x1, waiting for transfers between devices: 66.5 us -> 72 us  [body(): half_act = lax.all_gather(quant_act, CHIPS, axis=0, tiled=True)]
    all_to_all x1, starting transfers between devices: 11 us -> 5.48 us  [body(): lax.all_to_all(chip_sum.astype(jnp.bfloat16), CHIPS, 0, 0, tiled=True)]
  transfers between devices with their start and end apart: 10 -> 10, of which waited for: 4 -> 4; matrix products, arithmetic and copies ran while one was open for 12% -> 15% of each run, Pallas kernels for 0% -> 0%
where the time goes in v1:
time: 328 us; the launch traced here: 327 us
  waiting for transfers between devices  205 us (62%)
  matrix products  29 us (9%)
  other arithmetic  28.5 us (9%)
  starting transfers between devices  22.2 us (7%)
  blocking collectives  19.5 us (6%)
  between operations  15.6 us (5%)
  local copies, waits for them, and re-layouts  7.27 us (2%)
    all_gather x1, waiting for transfers between devices, body(): slots = jnp.sum(lax.all_gather(slots, DP + ('tensor',)), axis=0)  94.3 us
    all_gather x1, waiting for transfers between devices, body(): half_act = lax.all_gather(quant_act, CHIPS, axis=0, tiled=True)  72 us
    all_to_all x1, waiting for transfers between devices, body(): lax.all_to_all(chip_sum.astype(jnp.bfloat16), CHIPS, 0, 0, tiled=True)  36.2 us
    dot_general x1, matrix products, body(): lax.dot_general(all_act, all_cot, (((0,), (0,)), ((), ())), preferred_ele...  12.4 us
    all_gather x1, blocking collectives, body(): all_cot = lax.all_gather(cotangent, 'tensor', axis=0, tiled=True)  11.8 us
    reduce_sum x1, other arithmetic, body(): slots = jnp.sum(lax.all_gather(slots, DP + ('tensor',)), axis=0)  8.81 us
    dot_general x1, matrix products, body(): lax.dot_general(all_cot, quant_weight, (((1,), (1,)), ((), ())), preferre...  8.43 us
    ppermute x4, starting transfers between devices, swapped(): return lax.ppermute(block, axis, route)  7.77 us
  transfers between devices with their start and end apart: 10, of which 4 were waited for; matrix products, arithmetic and copies ran while one was open for 15% of the time, Pallas kernels for 0%

profile of v1, /device:TPU:1, one launch (start us, length us, event | category | flops | bytes accessed | tf_op | source)
XLA Modules:
  0.0 327.4 jit_solution(4944738131374757998)
XLA Ops:
  8.0 0.0 all-gather.3.cloned.1.call-start
  8.0 1.0 reshape.43
  9.1 0.3 convolution_bitcast_fusion.1
  9.4 0.4 convolution_multiply_fusion.1
  9.8 0.1 mul.67
  9.9 0.0 copy-start.2
  9.9 2.2 collective-permute-start
  12.1 7.3 %multiply_convert_fusion.1 = bf16[4096,768]{1,0:T(8,128)(2,1)} fusion(f32[768]{0:T(1024)} %param.8, bf16[4096,768]{1,0:T(8,128)(2,1)} %param.7), kind=kLoop, calls=%fused_computation.3 | loop fusion | flops 12582912 | bytes 12585984 | tf_op jit(solution)/shard_map/convert_element_type | solution.py:63
  19.4 0.0 copy-done.2
  19.4 11.8 %all_gather.12 = bf16[512,768]{1,0:T(8,128)(2,1)S(1)} all-gather(bf16[128,768]{1,0:T(8,128)(2,1)S(1)} %copy-done.2), channel_id=1, replica_groups=mesh['dx'=4,'dz'=8,'dc'=2,'tensor'=4] {'tensor'}, dimensions={0}, use_global_device_ids=true | all-gather | bytes 983040 | tf_op jit(solution)/shard_map/all_gather | solution.py:64
  31.2 0.0 collective-permute-done
  31.2 0.0 copy-start.3
  31.2 1.3 collective-permute-start.1
  32.5 8.4 %fusion.35 = f32[4096,512]{0,1:T(8,128)} fusion(bf16[4096,768]{1,0:T(8,128)(2,1)} %multiply_convert_fusion.1, bf16[512,768]{1,0:T(8,128)(2,1)S(1)} %all_gather.12), kind=kOutput, calls=%fused_computation.57 | convolution fusion | flops 3221225472 | bytes 15466496 | tf_op jit(solution)/shard_map/dot_general | solution.py:65
  40.9 0.0 collective-permute-done.1
  40.9 0.0 copy-done.3
  40.9 0.7 multiply_convert_fusion.2
  41.6 0.0 all-gather.3.cloned.1.call-update
  41.7 2.5 fusion.1
  44.1 3.5 %collective-permute-start.3 = (bf16[32,8,4096]{2,1,0:T(8,128)(2,1)S(1)}, bf16[32,8,4096]{2,1,0:T(8,128)(2,1)}, u32[]{:S(2)}, u32[]{:S(2)}) collective-permute-start(bf16[32,8,4096]{2,1,0:T(8,128)(2,1)S(1)} %fusion.1), channel_id=1, source_target_pairs={{0,4},{4,0},{1,5},{5,1},{2,6},{6,2},{3,7},{7,3},{8,12},{12,8},{9,1... | collective-permute-start | bytes 6291464 | tf_op jit(solution)/shard_map/ppermute | solution.py:92
  47.7 72.0 %all-gather.3.cloned.1.call-done = bf16[256,4096]{1,0:T(8,128)(2,1)} async-done(((bf16[8,4096]{1,0:T(8,128)(2,1)}), bf16[256,4096]{1,0:T(8,128)(2,1)}) %all-gather.3.cloned.1.call-update) | async-done | bytes 2097168 | tf_op jit(solution)/shard_map/all_gather | solution.py:69
  119.7 5.3 %collective-permute-start.2 = (bf16[256,4096]{1,0:T(8,128)(2,1)}, bf16[256,4096]{1,0:T(8,128)(2,1)}, u32[]{:S(2)}, u32[]{:S(2)}) collective-permute-start(bf16[256,4096]{1,0:T(8,128)(2,1)} %all-gather.3.cloned.1.call-done), channel_id=1, source_target_pairs={{0,4},{4,0},{1,5},{5,1},{2,6},{6,2},{3,7},{7,3},{8,12},{12,8},{9,1... | collective-permute-start | bytes 6291464 | tf_op jit(solution)/shard_map/ppermute | solution.py:71
  125.0 0.0 collective-permute-done.3
  125.0 4.7 %fusion = bf16[32,8,4096]{2,1,0:T(8,128)(2,1)} fusion(bf16[32,8,4096]{2,1,0:T(8,128)(2,1)} %collective-permute-done.3, f32[32,2,8,4096]{3,2,1,0:T(8,128)} %bitcast.42, s32[]{:T(128)S(6)} %select_n.50), kind=kLoop, calls=%fused_computation.7 | loop fusion | flops 3145728 | bytes 8388612 | tf_op jit(solution)/shard_map/convert_element_type | solution.py:93
  129.7 5.5 %all-to-all-start = ((bf16[32,8,4096]{2,1,0:T(8,128)(2,1)}), bf16[32,8,4096]{2,1,0:T(8,128)(2,1)S(1)}, u32[]{:S(2)}, u32[]{:S(2)}) async-start(bf16[32,8,4096]{2,1,0:T(8,128)(2,1)} %fusion), calls=%async_computation.1 | async-start | bytes 4194304 | tf_op jit(solution)/shard_map/all_to_all | solution.py:93
  135.2 0.0 reduce-scatter.2.cloned.1.call-start
  135.3 0.0 collective-permute-done.2
  135.3 4.2 %maximum_select_fusion = bf16[2,32,8,4096]{3,2,0,1:T(8,128)(2,1)S(1)} fusion(bf16[1,32,8,4096]{3,2,0,1:T(8,128)(2,1)} %bitcast.6, bf16[1,32,8,4096]{3,2,0,1:T(8,128)(2,1)} %bitcast.45, pred[]{:T(512)S(6)} %eq.11), kind=kLoop, calls=%fused_computation.5 | loop fusion | flops 6291456 | bytes 8388609 | tf_op jit(solution)/shard_map/jit(_where)/select_n | solution.py:72
  139.5 0.0 copy-start
  139.5 1.9 copy-done
  141.4 6.6 %fusion.36 = f32[512,768]{1,0:T(8,128)} fusion(bf16[512,4096]{1,0:T(8,128)(2,1)S(1)} %bitcast.43, bf16[4096,768]{1,0:T(8,128)(2,1)} %multiply_convert_fusion.1), kind=kOutput, calls=%fused_computation.58 | convolution fusion | flops 3221225472 | bytes 12058624 | tf_op jit(solution)/shard_map/dot_general | solution.py:78
  148.1 0.0 copy-start.4
  148.1 0.0 reduce-scatter.2.cloned.1.call-update
  148.1 0.0 all-gather.5.cloned.1.call-start
  148.1 36.2 %all-to-all-done = bf16[32,8,4096]{2,1,0:T(8,128)(2,1)S(1)} async-done(((bf16[32,8,4096]{2,1,0:T(8,128)(2,1)}), bf16[32,8,4096]{2,1,0:T(8,128)(2,1)S(1)}, u32[]{:S(2)}, u32[]{:S(2)}) %all-to-all-start) | async-done | bytes 2097184 | tf_op jit(solution)/shard_map/all_to_all | solution.py:93
  184.4 0.3 convert_reduce_fusion
  184.7 0.1 multiply_reduce_fusion.1
  184.8 0.2 dynamic_update_slice.5
  185.0 0.0 copy-start.1
  185.0 0.6 copy-done.1
  185.7 0.0 all-gather.5.cloned.1.call-update
  185.7 0.1 reshape.46
  185.8 0.4 convolution_bitcast_fusion
  186.2 0.4 convolution_multiply_fusion
  186.6 0.1 mul.74
  186.7 1.3 collective-permute-start.4
  188.0 2.6 collective-permute-done.4
  190.6 3.0 collective-permute-start.5
  193.7 0.0 copy-done.4
  193.7 12.4 %multiply_reduce_fusion = (f32[768]{0:T(1024)S(1)}, bf16[4096,768]{1,0:T(8,128)(2,1)}) fusion(f32[768]{0:T(1024)S(1)} %copy-done.4, bf16[4096,768]{1,0:T(8,128)(2,1)} %param.7, bf16[512,4096]{1,0:T(8,128)(2,1)} %bitcast.44, bf16[512,768]{1,0:T(8,128)(2,1)S(1)} %all_gather.12), kind=kOutput, calls=%fused_computation | convolution fusion | flops 3252681984 | bytes 17569792 | tf_op jit(solution)/shard_map/dot_general | solution.py:83
  206.1 7.7 %psum.7 = f32[768]{0:T(1024)} all-reduce(f32[768]{0:T(1024)S(1)} %get-tuple-element.11), channel_id=1, replica_groups=mesh['dx'=4,'dz'=8,'dc'=2,'tensor'=4] {'tensor'}, use_global_device_ids=true, to_apply=%region_5.6 | all-reduce | flops 768 | bytes 6144 | tf_op jit(solution)/shard_map/psum | solution.py:89
  213.8 0.0 collective-permute-done.5
  213.8 0.6 select_convert_fusion
  214.5 0.0 reduce-scatter.2.cloned.1.call-done
  214.5 1.7 convert_element_type.50
  216.2 94.3 %all-gather.5.cloned.1.call-done = f32[256,4,4096]{2,1,0:T(4,128)} async-done(((f32[1,4,4096]{2,1,0:T(4,128)}), f32[256,4,4096]{2,1,0:T(4,128)}) %all-gather.5.cloned.1.call-update) | async-done | bytes 16777232 | tf_op jit(solution)/shard_map/all_gather | solution.py:99
  310.5 8.8 %reduce_sum.38 = f32[4,4096]{1,0:T(4,128)S(1)} reduce(f32[256,4,4096]{2,1,0:T(4,128)} %all-gather.5.cloned.1.call-done, f32[]{:T(128)} %constant.45.clone.1), dimensions={0}, to_apply=%region_3.4 | reduce | flops 4177920 | bytes 16842756 | tf_op jit(solution)/shard_map/reduce_sum | solution.py:99
  319.3 0.6 constant_dynamic-slice_fusion
  (3 shorter events, 0.0 us)
Async XLA Ops:
  8.0 111.7 %all-gather.3.cloned.1.call-start = ((), (), s32[]{:S(2)}) async-start(), calls=%async_computation.2 | async-start | bytes 2162688 | tf_op jit(solution)/shard_map/all_gather | solution.py:69
  9.9 9.5 %copy-start.2 = (bf16[128,768]{1,0:T(8,128)(2,1)S(1)}, bf16[128,768]{1,0:T(8,128)(2,1)}, u32[]{:S(2)}) copy-start(bf16[128,768]{1,0:T(8,128)(2,1)} %param.9) | copy-start | bytes 589828
  9.9 21.3 %collective-permute-start = (f32[8,4096]{1,0:T(8,128)S(1)}, f32[8,4096]{1,0:T(8,128)S(1)}, u32[]{:S(2)}, u32[]{:S(2)}) collective-permute-start(f32[8,4096]{1,0:T(8,128)S(1)} %mul.67), channel_id=1, source_target_pairs={{0,1},{1,0},{2,3},{3,2},{4,5},{5,4},{6,7},{7,6},{8,9},{9,8},{10,11... | collective-permute-start | bytes 393224 | tf_op jit(solution)/shard_map/ppermute | solution.py:15
  31.2 9.7 %copy-start.3 = (f32[4096]{0:T(1024)S(1)}, f32[4096]{0:T(1024)}, u32[]{:S(2)}) copy-start(f32[4096]{0:T(1024)} %param.6) | copy-start | bytes 49156
  31.2 9.7 %collective-permute-start.1 = (f32[8,4096]{1,0:T(8,128)S(1)}, f32[8,4096]{1,0:T(8,128)S(1)}, u32[]{:S(2)}, u32[]{:S(2)}) collective-permute-start(f32[8,4096]{1,0:T(8,128)S(1)} %add_select_fusion.1), channel_id=1, source_target_pairs={{0,2},{2,0},{1,3},{3,1},{4,6},{6,4},{5,7},{7,5},{8,10},{10,8},{9,1... | collective-permute-start | bytes 393224 | tf_op jit(solution)/shard_map/ppermute | solution.py:15
  44.1 80.9 %collective-permute-start.3 = (bf16[32,8,4096]{2,1,0:T(8,128)(2,1)S(1)}, bf16[32,8,4096]{2,1,0:T(8,128)(2,1)}, u32[]{:S(2)}, u32[]{:S(2)}) collective-permute-start(bf16[32,8,4096]{2,1,0:T(8,128)(2,1)S(1)} %fusion.1), channel_id=1, source_target_pairs={{0,4},{4,0},{1,5},{5,1},{2,6},{6,2},{3,7},{7,3},{8,12},{12,8},{9,1... | collective-permute-start | bytes 6291464 | tf_op jit(solution)/shard_map/ppermute | solution.py:92
  119.7 15.6 %collective-permute-start.2 = (bf16[256,4096]{1,0:T(8,128)(2,1)}, bf16[256,4096]{1,0:T(8,128)(2,1)}, u32[]{:S(2)}, u32[]{:S(2)}) collective-permute-start(bf16[256,4096]{1,0:T(8,128)(2,1)} %all-gather.3.cloned.1.call-done), channel_id=1, source_target_pairs={{0,4},{4,0},{1,5},{5,1},{2,6},{6,2},{3,7},{7,3},{8,12},{12,8},{9,1... | collective-permute-start | bytes 6291464 | tf_op jit(solution)/shard_map/ppermute | solution.py:71
  129.7 54.6 %all-to-all-start = ((bf16[32,8,4096]{2,1,0:T(8,128)(2,1)}), bf16[32,8,4096]{2,1,0:T(8,128)(2,1)S(1)}, u32[]{:S(2)}, u32[]{:S(2)}) async-start(bf16[32,8,4096]{2,1,0:T(8,128)(2,1)} %fusion), calls=%async_computation.1 | async-start | bytes 4194304 | tf_op jit(solution)/shard_map/all_to_all | solution.py:93
  135.2 79.3 %reduce-scatter.2.cloned.1.call-start = ((), (), s32[]{:S(2)}) async-start(), calls=%async_computation.3 | async-start | bytes 1966080 | tf_op jit(solution)/shard_map/reduce_scatter | solution.py:77
  139.5 1.9 copy-start
  148.1 45.6 %copy-start.4 = (f32[768]{0:T(1024)S(1)}, f32[768]{0:T(1024)}, u32[]{:S(2)}) copy-start(f32[768]{0:T(1024)} %param.8) | copy-start | bytes 9220
  148.1 162.4 %all-gather.5.cloned.1.call-start = ((), (), s32[]{:S(2)}) async-start(), calls=%async_computation.4 | async-start | bytes 16842752 | tf_op jit(solution)/shard_map/all_gather | solution.py:99
  185.0 0.6 copy-start.1
  186.7 3.9 %collective-permute-start.4 = (f32[8,4096]{1,0:T(8,128)S(1)}, f32[8,4096]{1,0:T(8,128)S(1)}, u32[]{:S(2)}, u32[]{:S(2)}) collective-permute-start(f32[8,4096]{1,0:T(8,128)S(1)} %mul.74), channel_id=1, source_target_pairs={{0,1},{1,0},{2,3},{3,2},{4,5},{5,4},{6,7},{7,6},{8,9},{9,8},{10,11... | collective-permute-start | bytes 393224 | tf_op jit(solution)/shard_map/ppermute | solution.py:15
  190.6 23.2 %collective-permute-start.5 = (f32[8,4096]{1,0:T(8,128)S(1)}, f32[8,4096]{1,0:T(8,128)S(1)}, u32[]{:S(2)}, u32[]{:S(2)}) collective-permute-start(f32[8,4096]{1,0:T(8,128)S(1)} %add_select_fusion), channel_id=1, source_target_pairs={{0,2},{2,0},{1,3},{3,1},{4,6},{6,4},{5,7},{7,5},{8,10},{10,8},{9,1... | collective-permute-start | bytes 393224 | tf_op jit(solution)/shard_map/ppermute | solution.py:15
Sparse Core Ops, SparseCore 0:
  41.8 77.8 all-gather.2
  148.2 28.2 reduce-scatter.1
Sparse Core Ops, SparseCore 1:
  185.8 124.7 all-gather.4
